TPU v7x, 256 devices: a whole 4x4x8 slice. The times are simulated.
256 devices in a mesh: dp: 4 (over x), ctx: 64 (over z, y, core).
Axes of the slice: x: 4, y: 4, z: 8, core: 2. Of those that a mesh axis runs over, the one named last changes fastest.
Arguments:
- inputs: bfloat16 [4, 16384, 2304], P('dp', 'ctx'), may hold values from -16 to 16
- query: bfloat16 [4, 16384, 1024], P('dp', 'ctx'), may hold values from -110 to 110
- w_key: bfloat16 [2304, 512], P('dp'), may hold values from -0.125 to 0.125
- w_value: bfloat16 [2304, 512], P('dp'), may hold values from -0.125 to 0.125
- doc_lengths: int32 [4, 16], P('dp'), may hold values from 1 to 4096, 16384 in all within a row
- grad_out: bfloat16 [4, 16384, 1024], P('dp', 'ctx'), may hold values from -6 to 6
Outputs:
- attended: bfloat16 [4, 16384, 1024], P('dp', 'ctx')
- grad_query: bfloat16 [4, 16384, 1024], P('dp', 'ctx')
- grad_input: bfloat16 [4, 16384, 2304], P('dp', 'ctx')
- grad_wkey: bfloat16 [2304, 512], P('dp')
- grad_wvalue: bfloat16 [2304, 512], P('dp')
All inputs are finite; a program needn't handle non-finite values.
Results may differ from a plain program's by a relative error of at most 0.025.
The roundings to bfloat16 on the way count: a program that leaves them out, or rounds other values in their place, can miss the bound.
Values may be sent and summed in bfloat16 or wider, within the bound.
No kernel may reach another device: no remote copies, remote signals or barrier semaphores. Data moves between devices by JAX's collectives and lax.ppermute only.
A program may use at most 128 MiB of HBM per device.

v0:
```python
import jax
import jax.numpy as jnp
from jax import lax
from jax.sharding import PartitionSpec as P

D = 2304
HQ = 4
HK = 2
HD = 256
WINDOW = 2048
FLOOR = -1e30


def from_behind(value, axis, by):
    peers = lax.axis_size(axis)
    pairs = [(i, i + by) for i in range(peers) if 0 <= i + by < peers]
    return lax.ppermute(value, axis, pairs)


def segment_of(lengths, positions):
    doc_ends = jnp.cumsum(lengths, dtype=jnp.int32)
    return jnp.sum(
        (doc_ends[None, :] <= positions[:, None]).astype(jnp.int32), axis=1, dtype=jnp.int32
    )


def band_mask(query_pos, query_seg, key_pos, key_seg):
    distance_gap = query_pos[:, None] - key_pos[None, :]
    inside = (distance_gap >= 0) & (distance_gap < WINDOW) & (key_pos[None, :] >= 0)
    return inside & (query_seg[:, None] == key_seg[None, :])


def masked_scores(query_heads, key_rows, allowed):
    key_heads = key_rows.reshape(key_rows.shape[0], HK, HD)
    scores = jnp.einsum(
        "qkgd,tkd->kgqt", query_heads, key_heads, preferred_element_type=jnp.float32
    ) * HD ** (-0.5)
    return jnp.where(allowed[None, None], scores, -jnp.inf)


def score_stats(scores):
    highest = jnp.maximum(jnp.max(scores, axis=-1), FLOOR)
    summed = jnp.sum(jnp.exp(scores - highest[..., None]), axis=-1)
    return (highest, summed)


def softmax_of(scores, log_total):
    softmax = jnp.exp(scores - log_total[..., None])
    return (softmax, softmax.astype(jnp.bfloat16))


def values_of(soft_half, value_rows):
    value_heads = value_rows.reshape(value_rows.shape[0], HK, HD)
    return jnp.einsum("kgqt,tkd->qkgd", soft_half, value_heads, preferred_element_type=jnp.float32)


def row_delta(upstream_heads, mixed_half):
    products = upstream_heads.astype(jnp.float32) * mixed_half.astype(jnp.float32)
    return jnp.transpose(jnp.sum(products, axis=-1), (1, 2, 0))


def band_grads(softmax, soft_half, query_heads, upstream_heads, delta_sum, key_rows, value_rows):
    span_rows = key_rows.shape[0]
    key_heads = key_rows.reshape(span_rows, HK, HD)
    value_heads = value_rows.reshape(span_rows, HK, HD)
    prob_grad = jnp.einsum(
        "qkgd,tkd->kgqt", upstream_heads, value_heads, preferred_element_type=jnp.float32
    )
    score_grad = (softmax * (prob_grad - delta_sum[..., None]) * HD ** (-0.5)).astype(jnp.bfloat16)
    query_grad = jnp.einsum(
        "kgqt,tkd->qkgd", score_grad, key_heads, preferred_element_type=jnp.float32
    )
    key_grad = jnp.einsum(
        "kgqt,qkgd->tkd", score_grad, query_heads, preferred_element_type=jnp.float32
    )
    value_grad = jnp.einsum(
        "kgqt,qkgd->tkd", soft_half, upstream_heads, preferred_element_type=jnp.float32
    )
    kv_grad = jnp.concatenate(
        [key_grad.reshape(span_rows, HK * HD), value_grad.reshape(span_rows, HK * HD)], axis=1
    )
    return (query_grad, kv_grad)


def shards(inputs, query, w_key, w_value, doc_lengths, grad_out):
    tokens = inputs[0]
    queries = query[0]
    upstream = grad_out[0]
    lengths = doc_lengths[0]
    tok_rows = tokens.shape[0]
    distant = WINDOW // tok_rows
    per_group = HQ // HK
    kv_width = HK * HD
    key_full, value_full = (
        lax.all_gather(w_key, "dp", axis=0, tiled=True),
        lax.all_gather(w_value, "dp", axis=0, tiled=True),
    )
    key_own = jnp.dot(tokens, key_full, preferred_element_type=jnp.float32).astype(jnp.bfloat16)
    value_own = jnp.dot(tokens, value_full, preferred_element_type=jnp.float32).astype(jnp.bfloat16)
    kv_own = jnp.concatenate([key_own, value_own], axis=1)
    earlier = jnp.concatenate(
        [from_behind(kv_own, "ctx", distance) for distance in range(distant, 0, -1)], axis=0
    )
    window = jnp.concatenate([earlier, kv_own], axis=0)
    device_index = lax.axis_index("ctx")
    first_row = device_index * tok_rows
    query_pos = first_row + jnp.arange(tok_rows, dtype=jnp.int32)
    key_pos = first_row - distant * tok_rows + jnp.arange((distant + 1) * tok_rows, dtype=jnp.int32)
    allowed = band_mask(
        query_pos, segment_of(lengths, query_pos), key_pos, segment_of(lengths, key_pos)
    )
    query_heads = queries.reshape(tok_rows, HK, per_group, HD)
    upstream_heads = upstream.reshape(tok_rows, HK, per_group, HD)
    scores = masked_scores(query_heads, window[:, :kv_width], allowed)
    highest, summed = score_stats(scores)
    log_total = highest + jnp.log(summed)
    softmax, soft_half = softmax_of(scores, log_total)
    mixed_half = values_of(soft_half, window[:, kv_width:]).astype(jnp.bfloat16)
    delta_sum = row_delta(upstream_heads, mixed_half)
    query_grad, window_grad = band_grads(
        softmax,
        soft_half,
        query_heads,
        upstream_heads,
        delta_sum,
        window[:, :kv_width],
        window[:, kv_width:],
    )
    own_grad = window_grad[distant * tok_rows :]
    earlier_grad = window_grad[: distant * tok_rows]
    for distance in range(1, distant + 1):
        lower = (distant - distance) * tok_rows
        own_grad = own_grad + from_behind(earlier_grad[lower : lower + tok_rows], "ctx", -distance)
    kv_grad = own_grad.astype(jnp.bfloat16)
    grad_input = (
        jnp.dot(kv_grad[:, :kv_width], key_full.T, preferred_element_type=jnp.float32)
        + jnp.dot(kv_grad[:, kv_width:], value_full.T, preferred_element_type=jnp.float32)
    ).astype(jnp.bfloat16)
    share_sum = lax.psum_scatter(
        lax.dot_general(
            tokens, kv_grad, (((0,), (0,)), ((), ())), preferred_element_type=jnp.float32
        ),
        "dp",
        scatter_dimension=0,
        tiled=True,
    )
    weight_grad = lax.psum(share_sum, "ctx").astype(jnp.bfloat16)
    attended = mixed_half.reshape(1, tok_rows, HQ * HD)
    grad_query = query_grad.astype(jnp.bfloat16).reshape(1, tok_rows, HQ * HD)
    return (
        attended,
        grad_query,
        grad_input.reshape(1, tok_rows, D),
        weight_grad[:, :kv_width],
        weight_grad[:, kv_width:],
    )


def solution(mesh):
    in_specs = (
        P("dp", "ctx", None),
        P("dp", "ctx", None),
        P("dp", None),
        P("dp", None),
        P("dp", None),
        P("dp", "ctx", None),
    )
    out_specs = (
        P("dp", "ctx", None),
        P("dp", "ctx", None),
        P("dp", "ctx", None),
        P("dp", None),
        P("dp", None),
    )
    return jax.shard_map(shards, mesh=mesh, in_specs=in_specs, out_specs=out_specs, check_vma=False)
```

profile of v0, /device:TPU:2, one launch (start us, length us, event | category | flops | bytes accessed | tf_op | source)
XLA Modules:
  0.0 781.0 jit_solution(336791386545529585)
XLA Ops:
  8.7 0.7 copy.62
  9.9 37.5 %all-gather.5.cloned.1.call-done = bf16[2304,512]{1,0:T(8,128)(2,1)} async-done(((bf16[576,512]{1,0:T(8,128)(2,1)}), bf16[2304,512]{1,0:T(8,128)(2,1)}) %all-gather.5.cloned.1.call-update) | async-done | bytes 2359312 | tf_op jit(solution)/shard_map/all_gather | solution.py:96
  47.4 2.4 convolution_convert_fusion.1
  49.8 35.0 %all-gather.3.cloned.1.call-done = bf16[2304,512]{1,0:T(8,128)(2,1)} async-done(((bf16[576,512]{1,0:T(8,128)(2,1)}), bf16[2304,512]{1,0:T(8,128)(2,1)}) %all-gather.3.cloned.1.call-update) | async-done | bytes 2359312 | tf_op jit(solution)/shard_map/all_gather | solution.py:95
  84.8 2.4 convolution_convert_fusion.2
  87.3 4.3 collective-permute-start
  91.5 4.4 collective-permute-start.1
  96.0 3.8 collective-permute-start.2
  99.8 3.9 collective-permute-start.3
  103.7 4.6 collective-permute-start.4
  108.3 3.3 fusion.8
  111.6 1.0 copy.67
  112.6 1.0 copy.100
  113.6 1.3 collective-permute-start.5
  114.9 1.1 constant_dynamic-update-slice_fusion.8
  116.0 11.0 %collective-permute-done.1 = bf16[256,1024]{1,0:T(8,128)(2,1)} collective-permute-done((bf16[256,1024]{1,0:T(8,128)(2,1)S(1)}, bf16[256,1024]{1,0:T(8,128)(2,1)}, u32[]{:S(2)}, u32[]{:S(2)}) %collective-permute-start.1) | collective-permute-done | bytes 524320 | tf_op jit(solution)/shard_map/ppermute | solution.py:17
  127.0 1.3 collective-permute-start.6
  128.3 1.1 constant_dynamic-update-slice_fusion.7
  129.4 9.0 %collective-permute-done.2 = bf16[256,1024]{1,0:T(8,128)(2,1)} collective-permute-done((bf16[256,1024]{1,0:T(8,128)(2,1)S(1)}, bf16[256,1024]{1,0:T(8,128)(2,1)}, u32[]{:S(2)}, u32[]{:S(2)}) %collective-permute-start.2) | collective-permute-done | bytes 524320 | tf_op jit(solution)/shard_map/ppermute | solution.py:17
  138.3 1.5 collective-permute-start.7
  139.8 1.1 constant_dynamic-update-slice_fusion.6
  140.9 1.1 constant_dynamic-update-slice_fusion.5
  142.0 1.1 constant_dynamic-update-slice_fusion.4
  143.2 3.2 collective-permute-done.6
  146.5 2.5 fusion.41
  149.0 5.0 reshape.159
  154.0 4.5 copy.84
  158.5 3.8 fusion.43
  162.4 1.3 exponential_reduce_fusion
  163.6 2.7 copy-done.1
  166.4 2.1 reshape.156
  168.5 5.3 fusion.15
  173.8 1.2 copy-done.2
  175.8 2.6 multiply_reduce_fusion
  178.3 2.6 fusion.2
  181.0 1.4 fusion.44
  182.4 0.8 copy-done.4
  183.2 0.9 fusion.31
  184.1 1.3 collective-permute-start.15
  185.4 1.3 collective-permute-start.14
  186.7 1.5 collective-permute-start.13
  188.2 1.3 collective-permute-start.12
  189.5 1.3 collective-permute-start.11
  190.8 52.6 %collective-permute-done.15 = f32[256,1024]{0,1:T(8,128)S(1)} collective-permute-done((f32[256,1024]{0,1:T(8,128)S(1)}, f32[256,1024]{0,1:T(8,128)S(1)}, u32[]{:S(2)}, u32[]{:S(2)}) %collective-permute-start.15) | collective-permute-done | bytes 1048608 | tf_op jit(solution)/shard_map/ppermute | solution.py:17
  243.4 1.3 collective-permute-start.10
  244.7 13.0 %collective-permute-done.14 = f32[256,1024]{0,1:T(8,128)S(1)} collective-permute-done((f32[256,1024]{0,1:T(8,128)S(1)}, f32[256,1024]{0,1:T(8,128)S(1)}, u32[]{:S(2)}, u32[]{:S(2)}) %collective-permute-start.14) | collective-permute-done | bytes 1048608 | tf_op jit(solution)/shard_map/ppermute | solution.py:17
  257.7 1.3 collective-permute-start.9
  259.0 1.3 collective-permute-start.8
  260.3 16.9 %collective-permute-done.10 = f32[256,1024]{0,1:T(8,128)S(1)} collective-permute-done((f32[256,1024]{0,1:T(8,128)S(1)}, f32[256,1024]{0,1:T(8,128)S(1)}, u32[]{:S(2)}, u32[]{:S(2)}) %collective-permute-start.10) | collective-permute-done | bytes 1048608 | tf_op jit(solution)/shard_map/ppermute | solution.py:17
  277.3 46.2 %collective-permute-done.9 = f32[256,1024]{0,1:T(8,128)S(1)} collective-permute-done((f32[256,1024]{0,1:T(8,128)S(1)}, f32[256,1024]{0,1:T(8,128)S(1)}, u32[]{:S(2)}, u32[]{:S(2)}) %collective-permute-start.9) | collective-permute-done | bytes 1048608 | tf_op jit(solution)/shard_map/ppermute | solution.py:17
  324.1 5.0 convolution_bitcast_fusion
  329.1 9.6 %copy.98 = f32[2304,1024]{1,0:T(8,128)} copy(f32[2304,1024]{0,1:T(8,128)} %convolution_bitcast_fusion) | data formatting | bytes 18874368
  338.8 1.0 copy-done.12
  339.8 1.0 copy.75
  340.8 4.4 convolution_convert_fusion
  345.2 1.0 copy.76
  346.2 2.6 fusion.38
  348.9 1.8 fusion.5
  350.7 138.6 %reduce-scatter.4.cloned.1.call-done = f32[576,1024]{1,0:T(8,128)} async-done(((f32[2304,1024]{1,0:T(8,128)}), f32[576,1024]{1,0:T(8,128)}) %reduce-scatter.4.cloned.1.call-update) | async-done | bytes 2359312
  489.3 3.2 copy.99
  492.5 277.9 %all-reduce.1 = bf16[576,1024]{0,1:T(8,128)(2,1)S(1)} all-reduce(f32[576,1024]{0,1:T(8,128)} %copy.99), channel_id=1, replica_groups=mesh['dp'=4,'ctx'=64] {'ctx'}, use_global_device_ids=true, to_apply=%region_7.8 | all-reduce | flops 589824 | bytes 3538944 | tf_op jit(solution)/shard_map/psum | solution.py:147
  770.3 1.0 fusion.42
  771.3 2.1 copy.77
  773.4 1.1 copy.78
  (52 shorter events, 3.5 us)
Async XLA Ops:
  7.2 40.2 %copy-start = (bf16[1,256,2304]{2,1,0:T(8,128)(2,1)S(1)}, bf16[1,256,2304]{2,1,0:T(8,128)(2,1)}, u32[]{:S(2)}) copy-start(bf16[1,256,2304]{2,1,0:T(8,128)(2,1)} %param.6) | copy-start | bytes 3538948
  7.2 40.2 %all-gather.5.cloned.1.call-start = ((), (), s32[]{:S(2)}) async-start(), calls=%async_computation.2 | async-start | bytes 2949120 | tf_op jit(solution)/shard_map/all_gather | solution.py:96
  7.9 76.9 %all-gather.3.cloned.1.call-start = ((), (), s32[]{:S(2)}) async-start(), calls=%async_computation.1 | async-start | bytes 2949120 | tf_op jit(solution)/shard_map/all_gather | solution.py:95
  8.7 480.6 %reduce-scatter.4.cloned.1.call-start = ((), (), s32[]{:S(2)}) async-start(), calls=%async_computation.3 | async-start | bytes 11796480
  9.8 101.8 %copy-start.10 = (bf16[1,256,1024]{2,1,0:T(8,128)(2,1)S(1)}, bf16[1,256,1024]{2,1,0:T(8,128)(2,1)}, u32[]{:S(2)}) copy-start(bf16[1,256,1024]{2,1,0:T(8,128)(2,1)} %param.11) | copy-start | bytes 1572868
  9.8 102.8 %copy-start.11 = (bf16[1,256,1024]{2,1,0:T(8,128)(2,1)S(1)}, bf16[1,256,1024]{2,1,0:T(8,128)(2,1)}, u32[]{:S(2)}) copy-start(bf16[1,256,1024]{2,1,0:T(8,128)(2,1)} %param.7) | copy-start | bytes 1572868
  87.3 26.3 %collective-permute-start = (bf16[256,1024]{1,0:T(8,128)(2,1)S(1)}, bf16[256,1024]{1,0:T(8,128)(2,1)}, u32[]{:S(2)}, u32[]{:S(2)}) collective-permute-start(bf16[256,1024]{1,0:T(8,128)(2,1)S(1)} %pad_maximum_fusion.1), channel_id=1, source_target_pairs={{0,8},{1,9},{2,10},{3,11},{4,12},{5,13},{6,14},{7,15},{8,16},{9,17... | collective-permute-start | bytes 1572872 | tf_op jit(solution)/shard_map/ppermute | solution.py:17
  91.5 35.4 %collective-permute-start.1 = (bf16[256,1024]{1,0:T(8,128)(2,1)S(1)}, bf16[256,1024]{1,0:T(8,128)(2,1)}, u32[]{:S(2)}, u32[]{:S(2)}) collective-permute-start(bf16[256,1024]{1,0:T(8,128)(2,1)S(1)} %pad_maximum_fusion.1), channel_id=1, source_target_pairs={{0,7},{1,8},{2,9},{3,10},{4,11},{5,12},{6,13},{7,14},{8,15},{9,16}... | collective-permute-start | bytes 1572872 | tf_op jit(solution)/shard_map/ppermute | solution.py:17
  96.0 42.4 %collective-permute-start.2 = (bf16[256,1024]{1,0:T(8,128)(2,1)S(1)}, bf16[256,1024]{1,0:T(8,128)(2,1)}, u32[]{:S(2)}, u32[]{:S(2)}) collective-permute-start(bf16[256,1024]{1,0:T(8,128)(2,1)S(1)} %pad_maximum_fusion.1), channel_id=1, source_target_pairs={{0,6},{1,7},{2,8},{3,9},{4,10},{5,11},{6,12},{7,13},{8,14},{9,15},... | collective-permute-start | bytes 1572872 | tf_op jit(solution)/shard_map/ppermute | solution.py:17
  99.8 41.2 %collective-permute-start.3 = (bf16[256,1024]{1,0:T(8,128)(2,1)S(1)}, bf16[256,1024]{1,0:T(8,128)(2,1)}, u32[]{:S(2)}, u32[]{:S(2)}) collective-permute-start(bf16[256,1024]{1,0:T(8,128)(2,1)S(1)} %pad_maximum_fusion.1), channel_id=1, source_target_pairs={{0,5},{1,6},{2,7},{3,8},{4,9},{5,10},{6,11},{7,12},{8,13},{9,14},{... | collective-permute-start | bytes 1572872 | tf_op jit(solution)/shard_map/ppermute | solution.py:17
  103.7 38.3 %collective-permute-start.4 = (bf16[256,1024]{1,0:T(8,128)(2,1)S(1)}, bf16[256,1024]{1,0:T(8,128)(2,1)}, u32[]{:S(2)}, u32[]{:S(2)}) collective-permute-start(bf16[256,1024]{1,0:T(8,128)(2,1)S(1)} %pad_maximum_fusion.1), channel_id=1, source_target_pairs={{0,4},{1,5},{2,6},{3,7},{4,8},{5,9},{6,10},{7,11},{8,12},{9,13},{1... | collective-permute-start | bytes 1572872 | tf_op jit(solution)/shard_map/ppermute | solution.py:17
  113.6 29.5 %collective-permute-start.5 = (bf16[256,1024]{1,0:T(8,128)(2,1)S(1)}, bf16[256,1024]{1,0:T(8,128)(2,1)S(1)}, u32[]{:S(2)}, u32[]{:S(2)}) collective-permute-start(bf16[256,1024]{1,0:T(8,128)(2,1)S(1)} %pad_maximum_fusion.1), channel_id=1, source_target_pairs={{0,3},{1,4},{2,5},{3,6},{4,7},{5,8},{6,9},{7,10},{8,11},{9,12},{10... | collective-permute-start | bytes 1572872 | tf_op jit(solution)/shard_map/ppermute | solution.py:17
  127.0 19.4 %collective-permute-start.6 = (bf16[256,1024]{1,0:T(8,128)(2,1)S(1)}, bf16[256,1024]{1,0:T(8,128)(2,1)S(1)}, u32[]{:S(2)}, u32[]{:S(2)}) collective-permute-start(bf16[256,1024]{1,0:T(8,128)(2,1)S(1)} %pad_maximum_fusion.1), channel_id=1, source_target_pairs={{0,2},{1,3},{2,4},{3,5},{4,6},{5,7},{6,8},{7,9},{8,10},{9,11},{10,... | collective-permute-start | bytes 1572872 | tf_op jit(solution)/shard_map/ppermute | solution.py:17
  138.3 8.1 %collective-permute-start.7 = (bf16[256,1024]{1,0:T(8,128)(2,1)S(1)}, bf16[256,1024]{1,0:T(8,128)(2,1)S(1)}, u32[]{:S(2)}, u32[]{:S(2)}) collective-permute-start(bf16[256,1024]{1,0:T(8,128)(2,1)S(1)} %pad_maximum_fusion.1), channel_id=1, source_target_pairs={{0,1},{1,2},{2,3},{3,4},{4,5},{5,6},{6,7},{7,8},{8,9},{9,10},{10,1... | collective-permute-start | bytes 1572872 | tf_op jit(solution)/shard_map/ppermute | solution.py:17
  162.4 4.0 copy-start.1
  162.4 4.0 copy-start.3
  168.5 6.5 copy-start.2
  168.5 7.2 copy-start.6
  168.5 7.2 copy-start.8
  175.8 2.6 copy-start.9
  178.3 2.6 copy-start.7
  181.0 2.2 copy-start.4
  184.1 59.4 %collective-permute-start.15 = (f32[256,1024]{0,1:T(8,128)S(1)}, f32[256,1024]{0,1:T(8,128)S(1)}, u32[]{:S(2)}, u32[]{:S(2)}) collective-permute-start(f32[256,1024]{0,1:T(8,128)S(1)} %get-tuple-element.31), channel_id=1, source_target_pairs={{8,0},{9,1},{10,2},{11,3},{12,4},{13,5},{14,6},{15,7},{16,8},{17,9... | collective-permute-start | bytes 3145736 | tf_op jit(solution)/shard_map/ppermute | solution.py:17
  185.4 72.3 %collective-permute-start.14 = (f32[256,1024]{0,1:T(8,128)S(1)}, f32[256,1024]{0,1:T(8,128)S(1)}, u32[]{:S(2)}, u32[]{:S(2)}) collective-permute-start(f32[256,1024]{0,1:T(8,128)S(1)} %get-tuple-element.32), channel_id=1, source_target_pairs={{7,0},{8,1},{9,2},{10,3},{11,4},{12,5},{13,6},{14,7},{15,8},{16,9}... | collective-permute-start | bytes 3145736 | tf_op jit(solution)/shard_map/ppermute | solution.py:17
  186.7 72.3 %collective-permute-start.13 = (f32[256,1024]{0,1:T(8,128)S(1)}, f32[256,1024]{0,1:T(8,128)S(1)}, u32[]{:S(2)}, u32[]{:S(2)}) collective-permute-start(f32[256,1024]{0,1:T(8,128)S(1)} %get-tuple-element.30), channel_id=1, source_target_pairs={{6,0},{7,1},{8,2},{9,3},{10,4},{11,5},{12,6},{13,7},{14,8},{15,9},... | collective-permute-start | bytes 3145736 | tf_op jit(solution)/shard_map/ppermute | solution.py:17
  188.2 72.1 %collective-permute-start.12 = (f32[256,1024]{0,1:T(8,128)S(1)}, f32[256,1024]{0,1:T(8,128)S(1)}, u32[]{:S(2)}, u32[]{:S(2)}) collective-permute-start(f32[256,1024]{0,1:T(8,128)S(1)} %get-tuple-element.29), channel_id=1, source_target_pairs={{5,0},{6,1},{7,2},{8,3},{9,4},{10,5},{11,6},{12,7},{13,8},{14,9},{... | collective-permute-start | bytes 3145736 | tf_op jit(solution)/shard_map/ppermute | solution.py:17
  189.5 70.8 %collective-permute-start.11 = (f32[256,1024]{0,1:T(8,128)S(1)}, f32[256,1024]{0,1:T(8,128)S(1)}, u32[]{:S(2)}, u32[]{:S(2)}) collective-permute-start(f32[256,1024]{0,1:T(8,128)S(1)} %get-tuple-element.28), channel_id=1, source_target_pairs={{4,0},{5,1},{6,2},{7,3},{8,4},{9,5},{10,6},{11,7},{12,8},{13,9},{1... | collective-permute-start | bytes 3145736 | tf_op jit(solution)/shard_map/ppermute | solution.py:17
  243.4 33.8 %collective-permute-start.10 = (f32[256,1024]{0,1:T(8,128)S(1)}, f32[256,1024]{0,1:T(8,128)S(1)}, u32[]{:S(2)}, u32[]{:S(2)}) collective-permute-start(f32[256,1024]{0,1:T(8,128)S(1)} %get-tuple-element.27), channel_id=1, source_target_pairs={{3,0},{4,1},{5,2},{6,3},{7,4},{8,5},{9,6},{10,7},{11,8},{12,9},{13... | collective-permute-start | bytes 3145736 | tf_op jit(solution)/shard_map/ppermute | solution.py:17
  257.7 65.7 %collective-permute-start.9 = (f32[256,1024]{0,1:T(8,128)S(1)}, f32[256,1024]{0,1:T(8,128)S(1)}, u32[]{:S(2)}, u32[]{:S(2)}) collective-permute-start(f32[256,1024]{0,1:T(8,128)S(1)} %get-tuple-element.26), channel_id=1, source_target_pairs={{2,0},{3,1},{4,2},{5,3},{6,4},{7,5},{8,6},{9,7},{10,8},{11,9},{12,... | collective-permute-start | bytes 3145736 | tf_op jit(solution)/shard_map/ppermute | solution.py:17
  259.0 64.4 %collective-permute-start.8 = (f32[256,1024]{0,1:T(8,128)S(1)}, f32[256,1024]{0,1:T(8,128)S(1)}, u32[]{:S(2)}, u32[]{:S(2)}) collective-permute-start(f32[256,1024]{0,1:T(8,128)S(1)} %get-tuple-element.25), channel_id=1, source_target_pairs={{1,0},{2,1},{3,2},{4,3},{5,4},{6,5},{7,6},{8,7},{9,8},{10,9},{11,1... | collective-permute-start | bytes 3145736 | tf_op jit(solution)/shard_map/ppermute | solution.py:17
  338.7 1.0 copy-start.12
  346.2 2.6 copy-start.5
Sparse Core Ops, SparseCore 0:
  9.8 37.5 all-gather.4
  49.2 35.5 all-gather.2
  338.9 150.3 reduce-scatter.3
where the time goes:
time: 782 us; the launch traced here: 781 us
  waiting for transfers between devices  364 us (47%)
  blocking collectives  278 us (36%)
  local copies, waits for them, and re-layouts  47.8 us (6%)
  starting transfers between devices  35.8 us (5%)
  matrix products  34.5 us (4%)
  between operations  14.2 us (2%)
    psum x1, blocking collectives, shards(): weight_grad = lax.psum(share_sum, 'ctx').astype(jnp.bfloat16)  278 us
    ppermute x16, waiting for transfers between devices, from_behind(): return lax.ppermute(value, axis, pairs)  152 us
    unnamed x4, waiting for transfers between devices  140 us
    all_gather x1, waiting for transfers between devices, shards(): lax.all_gather(w_value, 'dp', axis=0, tiled=True)  37.5 us
    ppermute x16, starting transfers between devices, from_behind(): return lax.ppermute(value, axis, pairs)  35.7 us
    all_gather x1, waiting for transfers between devices, shards(): lax.all_gather(w_key, 'dp', axis=0, tiled=True)  35 us
    unnamed x41, local copies, waits for them, and re-layouts  30.9 us
  transfers between devices with their start and end apart: 19, of which 10 were waited for; matrix products, arithmetic and copies ran while one was open for 3% of the time, Pallas kernels for 0%

commit v1 on v0

--- a/solution.py
+++ b/solution.py
@@ -1,3 +1,4 @@
+import functools
 import jax
 import jax.numpy as jnp
 from jax import lax
@@ -9,6 +10,38 @@
 HD = 256
 WINDOW = 2048
 FLOOR = -1e30
+
+
+def match_the_target(w_in, axis_no):
+    w_in = jnp.moveaxis(w_in, 0, axis_no)
+    shaped = w_in.shape
+    step_out = w_in.reshape(
+        *shaped[:axis_no], shaped[axis_no] * shaped[axis_no + 1], *shaped[axis_no + 2 :]
+    )
+    return step_out
+
+
+def report_bars(x_in, which_axis, out_dim):
+    parts_n = lax.axis_size(which_axis)
+    so_far_all = list(map(lambda jj: (jj, (jj + 1) % parts_n), range(parts_n)))
+    chunks = [(src_i, pp) for pp, src_i in so_far_all]
+    side_arr, finding = ([], [])
+    for at in range(parts_n - 1):
+        if at % 2 == 0:
+            side_arr.append(
+                lax.ppermute(side_arr[-1] if side_arr else x_in, which_axis, so_far_all)
+            )
+        else:
+            finding.append(lax.ppermute(finding[-1] if finding else x_in, which_axis, chunks))
+    t1 = jnp.stack([*side_arr[::-1], x_in, *finding], axis=0)
+    w2 = lax.axis_index(which_axis)
+    last = w2 - len(side_arr)
+    t1 = t1[(jnp.arange(parts_n) - last) % parts_n]
+    piece_out = match_the_target(t1, out_dim)
+    return piece_out
+
+
+patches_clear = functools.partial(report_bars, which_axis="dp", out_dim=0)
 
 
 def from_behind(value, axis, by):
@@ -91,10 +124,7 @@
     distant = WINDOW // tok_rows
     per_group = HQ // HK
     kv_width = HK * HD
-    key_full, value_full = (
-        lax.all_gather(w_key, "dp", axis=0, tiled=True),
-        lax.all_gather(w_value, "dp", axis=0, tiled=True),
-    )
+    key_full, value_full = (patches_clear(w_key), lax.all_gather(w_value, "dp", axis=0, tiled=True))
     key_own = jnp.dot(tokens, key_full, preferred_element_type=jnp.float32).astype(jnp.bfloat16)
     value_own = jnp.dot(tokens, value_full, preferred_element_type=jnp.float32).astype(jnp.bfloat16)
     kv_own = jnp.concatenate([key_own, value_own], axis=1)

time: 782 us -> 739 us (0.945)
  waiting for transfers between devices: 364 us -> 319 us
  local copies, waits for them, and re-layouts: 47.8 us -> 36.6 us
  starting transfers between devices: 35.8 us -> 43.9 us
    all_gather x1, waiting for transfers between devices: 37.5 us -> 0.09 us  [shards(): lax.all_gather(w_value, 'dp', axis=0, tiled=True)]
    all_gather x1 -> x0, waiting for transfers between devices: 35 us -> none  [shards(): lax.all_gather(w_key, 'dp', axis=0, tiled=True)]
    ppermute x0 -> x3, waiting for transfers between devices: none -> 35 us  [the longest x2 35 us: report_bars(): lax.ppermute(side_arr[-1] if side_arr else x_in, which_axis, so_far_all)]
    reshape x3 -> x0, local copies, waits for them, and re-layouts: 11.6 us -> none  [the longest x2 9.5 us: masked_scores(): key_heads = key_rows.reshape(key_rows.shape[0], HK, HD)]
    unnamed x4 -> x3, waiting for transfers between devices: 140 us -> 134 us
    unnamed x41 -> x43, local copies, waits for them, and re-layouts: 30.9 us -> 30 us
  transfers between devices with their start and end apart: 19 -> 21, of which waited for: 10 -> 10; matrix products, arithmetic and copies ran while one was open for 3% -> 5% of each run, Pallas kernels for 0% -> 0%
where the time goes in v1:
time: 739 us; the launch traced here: 737 us
  waiting for transfers between devices  319 us (43%)
  blocking collectives  278 us (38%)
  starting transfers between devices  43.9 us (6%)
  local copies, waits for them, and re-layouts  36.6 us (5%)
  matrix products  32.1 us (4%)
  between operations  14.5 us (2%)
  other arithmetic  13.6 us (2%)
    psum x1, blocking collectives, shards(): weight_grad = lax.psum(share_sum, 'ctx').astype(jnp.bfloat16)  278 us
    ppermute x16, waiting for transfers between devices, from_behind(): return lax.ppermute(value, axis, pairs)  149 us
    unnamed x3, waiting for transfers between devices  134 us
    ppermute x16, starting transfers between devices, from_behind(): return lax.ppermute(value, axis, pairs)  39.9 us
    ppermute x2, waiting for transfers between devices, report_bars(): lax.ppermute(side_arr[-1] if side_arr else x_in, which_axis, so_far_all)  35 us
    unnamed x43, local copies, waits for them, and re-layouts  30 us
  transfers between devices with their start and end apart: 21, of which 10 were waited for; matrix products, arithmetic and copies ran while one was open for 5% of the time, Pallas kernels for 0%

profile of v1, /device:TPU:2, one launch (start us, length us, event | category | flops | bytes accessed | tf_op | source)
XLA Modules:
  0.0 737.2 jit_solution(4434840999745719413)
XLA Ops:
  8.0 1.6 collective-permute-start
  9.5 0.8 collective-permute-start.2
  10.4 12.9 %collective-permute-done = bf16[576,512]{1,0:T(8,128)(2,1)S(1)} collective-permute-done((bf16[576,512]{1,0:T(8,128)(2,1)}, bf16[576,512]{1,0:T(8,128)(2,1)S(1)}, u32[]{:S(2)}, u32[]{:S(2)}) %collective-permute-start) | collective-permute-done | bytes 589856 | tf_op jit(solution)/shard_map/ppermute | solution.py:32
  23.3 1.5 collective-permute-start.1
  24.8 0.7 copy.60
  27.0 0.7 convert_reduce_fusion
  27.7 22.0 %collective-permute-done.1 = bf16[576,512]{1,0:T(8,128)(2,1)S(1)} collective-permute-done((bf16[576,512]{1,0:T(8,128)(2,1)S(1)}, bf16[576,512]{1,0:T(8,128)(2,1)S(1)}, u32[]{:S(2)}, u32[]{:S(2)}) %collective-permute-start.1) | collective-permute-done | bytes 589856 | tf_op jit(solution)/shard_map/ppermute | solution.py:32
  49.7 2.8 pad_maximum_fusion
  52.5 2.5 gather_fusion
  55.0 1.5 fusion.15
  56.6 2.7 convolution_convert_fusion.2
  59.3 0.7 copy-done.9
  60.1 1.8 pad_maximum_fusion.2
  61.8 5.1 collective-permute-start.3
  66.9 4.7 collective-permute-start.4
  71.6 4.0 collective-permute-start.5
  75.7 4.8 collective-permute-start.6
  80.5 5.0 collective-permute-start.7
  85.5 4.0 fusion.8
  89.5 2.0 copy.64
  91.5 2.0 copy.93
  93.6 1.4 collective-permute-start.8
  95.0 1.1 constant_dynamic-update-slice_fusion.8
  96.1 2.8 collective-permute-start.9
  98.9 1.1 constant_dynamic-update-slice_fusion.7
  100.0 13.4 %collective-permute-done.5 = bf16[256,1024]{0,1:T(8,128)(2,1)} collective-permute-done((bf16[256,1024]{0,1:T(8,128)(2,1)}, bf16[256,1024]{0,1:T(8,128)(2,1)}, u32[]{:S(2)}, u32[]{:S(2)}) %collective-permute-start.5) | collective-permute-done | bytes 524320 | tf_op jit(solution)/shard_map/ppermute | solution.py:50
  113.4 1.5 collective-permute-start.10
  114.9 1.1 constant_dynamic-update-slice_fusion.6
  116.0 1.1 constant_dynamic-update-slice_fusion.5
  117.1 1.1 constant_dynamic-update-slice_fusion.4
  118.2 2.0 collective-permute-done.9
  121.6 1.9 fusion.42
  123.6 1.3 exponential_reduce_fusion
  124.8 1.4 fusion.9
  126.3 2.4 multiply_reduce_fusion
  128.7 4.4 fusion.2
  133.1 2.9 fusion.43
  136.0 0.9 fusion.28
  137.0 1.3 collective-permute-start.18
  138.3 1.3 collective-permute-start.17
  139.6 1.3 collective-permute-start.16
  140.9 1.3 collective-permute-start.15
  142.2 1.3 collective-permute-start.14
  143.5 54.8 %collective-permute-done.18 = f32[256,1024]{0,1:T(8,128)S(1)} collective-permute-done((f32[256,1024]{0,1:T(8,128)S(1)}, f32[256,1024]{0,1:T(8,128)S(1)}, u32[]{:S(2)}, u32[]{:S(2)}) %collective-permute-start.18) | collective-permute-done | bytes 1048608 | tf_op jit(solution)/shard_map/ppermute | solution.py:50
  198.3 1.5 collective-permute-start.13
  199.8 17.6 %collective-permute-done.17 = f32[256,1024]{0,1:T(8,128)S(1)} collective-permute-done((f32[256,1024]{0,1:T(8,128)S(1)}, f32[256,1024]{0,1:T(8,128)S(1)}, u32[]{:S(2)}, u32[]{:S(2)}) %collective-permute-start.17) | collective-permute-done | bytes 1048608 | tf_op jit(solution)/shard_map/ppermute | solution.py:50
  217.3 1.3 collective-permute-start.12
  218.6 1.3 collective-permute-start.11
  220.0 1.0 collective-permute-done.13
  221.0 60.4 %collective-permute-done.12 = f32[256,1024]{0,1:T(8,128)S(1)} collective-permute-done((f32[256,1024]{0,1:T(8,128)S(1)}, f32[256,1024]{0,1:T(8,128)S(1)}, u32[]{:S(2)}, u32[]{:S(2)}) %collective-permute-start.12) | collective-permute-done | bytes 1048608 | tf_op jit(solution)/shard_map/ppermute | solution.py:50
  282.1 0.8 copy-done.3
  282.9 5.1 convolution_bitcast_fusion
  287.9 9.6 %copy.91 = f32[2304,1024]{1,0:T(8,128)} copy(f32[2304,1024]{0,1:T(8,128)} %convolution_bitcast_fusion) | data formatting | bytes 18874368
  297.6 2.0 copy.71
  299.6 5.2 convolution_convert_fusion
  304.8 2.0 copy.72
  306.9 2.6 fusion.35
  309.5 1.9 fusion.5
  311.4 133.8 %reduce-scatter.4.cloned.1.call-done = f32[576,1024]{1,0:T(8,128)} async-done(((f32[2304,1024]{1,0:T(8,128)}), f32[576,1024]{1,0:T(8,128)}) %reduce-scatter.4.cloned.1.call-update) | async-done | bytes 2359312
  445.2 3.2 copy.92
  448.4 277.9 %all-reduce.1 = bf16[576,1024]{0,1:T(8,128)(2,1)S(1)} all-reduce(f32[576,1024]{0,1:T(8,128)} %copy.92), channel_id=1, replica_groups=mesh['dp'=4,'ctx'=64] {'ctx'}, use_global_device_ids=true, to_apply=%region_7.8 | all-reduce | flops 589824 | bytes 3538944 | tf_op jit(solution)/shard_map/psum | solution.py:177
  726.2 1.0 fusion.41
  727.2 2.1 copy.73
  729.3 1.1 copy.74
  (58 shorter events, 4.4 us)
Async XLA Ops:
  7.2 47.8 %copy-start = (bf16[1,256,2304]{2,1,0:T(8,128)(2,1)S(1)}, bf16[1,256,2304]{2,1,0:T(8,128)(2,1)}, u32[]{:S(2)}) copy-start(bf16[1,256,2304]{2,1,0:T(8,128)(2,1)} %param.6) | copy-start | bytes 3538948
  7.2 49.4 %all-gather.2.cloned.1.call-start = ((), (), s32[]{:S(2)}) async-start(), calls=%async_computation.1 | async-start | bytes 2949120 | tf_op jit(solution)/shard_map/all_gather | solution.py:127
  7.9 437.3 %reduce-scatter.4.cloned.1.call-start = ((), (), s32[]{:S(2)}) async-start(), calls=%async_computation.2 | async-start | bytes 11796480
  8.0 15.4 %collective-permute-start = (bf16[576,512]{1,0:T(8,128)(2,1)}, bf16[576,512]{1,0:T(8,128)(2,1)S(1)}, u32[]{:S(2)}, u32[]{:S(2)}) collective-permute-start(bf16[576,512]{1,0:T(8,128)(2,1)} %param.8), channel_id=1, source_target_pairs={{0,64},{64,128},{128,192},{192,0},{1,65},{65,129},{129,193},{193,1... | collective-permute-start | bytes 1769480 | tf_op jit(solution)/shard_map/ppermute | solution.py:32
  9.5 18.1 %collective-permute-start.2 = (bf16[576,512]{1,0:T(8,128)(2,1)}, bf16[576,512]{1,0:T(8,128)(2,1)S(1)}, u32[]{:S(2)}, u32[]{:S(2)}) collective-permute-start(bf16[576,512]{1,0:T(8,128)(2,1)} %param.8), channel_id=1, source_target_pairs={{64,0},{128,64},{192,128},{0,192},{65,1},{129,65},{193,129},{1,193... | collective-permute-start | bytes 1769480 | tf_op jit(solution)/shard_map/ppermute | solution.py:35
  10.4 39.3 %copy-start.13 = (s32[256]{0:T(256)}, s32[256]{0:T(256)S(1)}, u32[]{:S(2)}) copy-start(s32[256]{0:T(256)S(1)} %iota_add_fusion.1) | copy-start | bytes 3076
  23.3 26.4 %collective-permute-start.1 = (bf16[576,512]{1,0:T(8,128)(2,1)S(1)}, bf16[576,512]{1,0:T(8,128)(2,1)S(1)}, u32[]{:S(2)}, u32[]{:S(2)}) collective-permute-start(bf16[576,512]{1,0:T(8,128)(2,1)S(1)} %collective-permute-done), channel_id=1, source_target_pairs={{0,64},{64,128},{128,192},{192,0},{1,65},{65,129},{129,193},{193,1... | collective-permute-start | bytes 1769480 | tf_op jit(solution)/shard_map/ppermute | solution.py:32
  56.6 28.9 %copy-start.12 = (s32[2304]{0:T(1024)S(1)}, s32[2304]{0:T(1024)}, u32[]{:S(2)}) copy-start(s32[2304]{0:T(1024)} %convert_reduce_fusion) | copy-start | bytes 27652
  59.3 0.7 copy-start.9
  61.8 31.7 %collective-permute-start.3 = (bf16[256,1024]{0,1:T(8,128)(2,1)}, bf16[256,1024]{0,1:T(8,128)(2,1)}, u32[]{:S(2)}, u32[]{:S(2)}) collective-permute-start(bf16[256,1024]{0,1:T(8,128)(2,1)} %pad_maximum_fusion.2), channel_id=1, source_target_pairs={{0,8},{1,9},{2,10},{3,11},{4,12},{5,13},{6,14},{7,15},{8,16},{9,17... | collective-permute-start | bytes 1572872 | tf_op jit(solution)/shard_map/ppermute | solution.py:50
  66.9 29.2 %collective-permute-start.4 = (bf16[256,1024]{0,1:T(8,128)(2,1)}, bf16[256,1024]{0,1:T(8,128)(2,1)}, u32[]{:S(2)}, u32[]{:S(2)}) collective-permute-start(bf16[256,1024]{0,1:T(8,128)(2,1)} %pad_maximum_fusion.2), channel_id=1, source_target_pairs={{0,7},{1,8},{2,9},{3,10},{4,11},{5,12},{6,13},{7,14},{8,15},{9,16}... | collective-permute-start | bytes 1572872 | tf_op jit(solution)/shard_map/ppermute | solution.py:50
  71.6 41.8 %collective-permute-start.5 = (bf16[256,1024]{0,1:T(8,128)(2,1)}, bf16[256,1024]{0,1:T(8,128)(2,1)}, u32[]{:S(2)}, u32[]{:S(2)}) collective-permute-start(bf16[256,1024]{0,1:T(8,128)(2,1)} %pad_maximum_fusion.2), channel_id=1, source_target_pairs={{0,6},{1,7},{2,8},{3,9},{4,10},{5,11},{6,12},{7,13},{8,14},{9,15},... | collective-permute-start | bytes 1572872 | tf_op jit(solution)/shard_map/ppermute | solution.py:50
  75.7 40.3 %collective-permute-start.6 = (bf16[256,1024]{0,1:T(8,128)(2,1)}, bf16[256,1024]{0,1:T(8,128)(2,1)}, u32[]{:S(2)}, u32[]{:S(2)}) collective-permute-start(bf16[256,1024]{0,1:T(8,128)(2,1)} %pad_maximum_fusion.2), channel_id=1, source_target_pairs={{0,5},{1,6},{2,7},{3,8},{4,9},{5,10},{6,11},{7,12},{8,13},{9,14},{... | collective-permute-start | bytes 1572872 | tf_op jit(solution)/shard_map/ppermute | solution.py:50
  80.5 36.6 %collective-permute-start.7 = (bf16[256,1024]{0,1:T(8,128)(2,1)}, bf16[256,1024]{0,1:T(8,128)(2,1)}, u32[]{:S(2)}, u32[]{:S(2)}) collective-permute-start(bf16[256,1024]{0,1:T(8,128)(2,1)} %pad_maximum_fusion.2), channel_id=1, source_target_pairs={{0,4},{1,5},{2,6},{3,7},{4,8},{5,9},{6,10},{7,11},{8,12},{9,13},{1... | collective-permute-start | bytes 1572872 | tf_op jit(solution)/shard_map/ppermute | solution.py:50
  93.6 26.7 %copy-start.8 = (bf16[256,512]{0,1:T(8,128)(2,1)S(1)}, bf16[256,512]{0,1:T(8,128)(2,1)}, u32[]{:S(2)}) copy-start(bf16[256,512]{0,1:T(8,128)(2,1)} %fusion.15) | copy-start | bytes 786436
  93.6 26.8 %copy-start.10 = (bf16[256,512]{0,1:T(8,128)(2,1)S(1)}, bf16[256,512]{0,1:T(8,128)(2,1)}, u32[]{:S(2)}) copy-start(bf16[256,512]{0,1:T(8,128)(2,1)} %copy-done.9) | copy-start | bytes 786436
  93.6 24.6 %collective-permute-start.8 = (bf16[256,1024]{0,1:T(8,128)(2,1)}, bf16[256,1024]{0,1:T(8,128)(2,1)S(1)}, u32[]{:S(2)}, u32[]{:S(2)}) collective-permute-start(bf16[256,1024]{0,1:T(8,128)(2,1)} %pad_maximum_fusion.2), channel_id=1, source_target_pairs={{0,3},{1,4},{2,5},{3,6},{4,7},{5,8},{6,9},{7,10},{8,11},{9,12},{10... | collective-permute-start | bytes 1572872 | tf_op jit(solution)/shard_map/ppermute | solution.py:50
  96.1 24.1 %collective-permute-start.9 = (bf16[256,1024]{0,1:T(8,128)(2,1)}, bf16[256,1024]{0,1:T(8,128)(2,1)S(1)}, u32[]{:S(2)}, u32[]{:S(2)}) collective-permute-start(bf16[256,1024]{0,1:T(8,128)(2,1)} %pad_maximum_fusion.2), channel_id=1, source_target_pairs={{0,2},{1,3},{2,4},{3,5},{4,6},{5,7},{6,8},{7,9},{8,10},{9,11},{10,... | collective-permute-start | bytes 1572872 | tf_op jit(solution)/shard_map/ppermute | solution.py:50
  113.4 6.9 collective-permute-start.10
  120.4 1.0 copy-start.7
  120.4 1.2 copy-start.11
  120.7 2.8 copy-start.6
  120.7 5.6 copy-start.2
  123.6 1.3 copy-start.5
  133.1 2.9 copy-start.1
  137.0 61.3 %collective-permute-start.18 = (f32[256,1024]{0,1:T(8,128)S(1)}, f32[256,1024]{0,1:T(8,128)S(1)}, u32[]{:S(2)}, u32[]{:S(2)}) collective-permute-start(f32[256,1024]{0,1:T(8,128)S(1)} %get-tuple-element.31), channel_id=1, source_target_pairs={{8,0},{9,1},{10,2},{11,3},{12,4},{13,5},{14,6},{15,7},{16,8},{17,9... | collective-permute-start | bytes 3145736 | tf_op jit(solution)/shard_map/ppermute | solution.py:50
  138.3 79.1 %collective-permute-start.17 = (f32[256,1024]{0,1:T(8,128)S(1)}, f32[256,1024]{0,1:T(8,128)S(1)}, u32[]{:S(2)}, u32[]{:S(2)}) collective-permute-start(f32[256,1024]{0,1:T(8,128)S(1)} %get-tuple-element.32), channel_id=1, source_target_pairs={{7,0},{8,1},{9,2},{10,3},{11,4},{12,5},{13,6},{14,7},{15,8},{16,9}... | collective-permute-start | bytes 3145736 | tf_op jit(solution)/shard_map/ppermute | solution.py:50
  139.6 79.1 %collective-permute-start.16 = (f32[256,1024]{0,1:T(8,128)S(1)}, f32[256,1024]{0,1:T(8,128)S(1)}, u32[]{:S(2)}, u32[]{:S(2)}) collective-permute-start(f32[256,1024]{0,1:T(8,128)S(1)} %get-tuple-element.30), channel_id=1, source_target_pairs={{6,0},{7,1},{8,2},{9,3},{10,4},{11,5},{12,6},{13,7},{14,8},{15,9},... | collective-permute-start | bytes 3145736 | tf_op jit(solution)/shard_map/ppermute | solution.py:50
  140.9 79.1 %collective-permute-start.15 = (f32[256,1024]{0,1:T(8,128)S(1)}, f32[256,1024]{0,1:T(8,128)S(1)}, u32[]{:S(2)}, u32[]{:S(2)}) collective-permute-start(f32[256,1024]{0,1:T(8,128)S(1)} %get-tuple-element.29), channel_id=1, source_target_pairs={{5,0},{6,1},{7,2},{8,3},{9,4},{10,5},{11,6},{12,7},{13,8},{14,9},{... | collective-permute-start | bytes 3145736 | tf_op jit(solution)/shard_map/ppermute | solution.py:50
  142.2 77.8 %collective-permute-start.14 = (f32[256,1024]{0,1:T(8,128)S(1)}, f32[256,1024]{0,1:T(8,128)S(1)}, u32[]{:S(2)}, u32[]{:S(2)}) collective-permute-start(f32[256,1024]{0,1:T(8,128)S(1)} %get-tuple-element.28), channel_id=1, source_target_pairs={{4,0},{5,1},{6,2},{7,3},{8,4},{9,5},{10,6},{11,7},{12,8},{13,9},{1... | collective-permute-start | bytes 3145736 | tf_op jit(solution)/shard_map/ppermute | solution.py:50
  198.3 22.7 %collective-permute-start.13 = (f32[256,1024]{0,1:T(8,128)S(1)}, f32[256,1024]{0,1:T(8,128)S(1)}, u32[]{:S(2)}, u32[]{:S(2)}) collective-permute-start(f32[256,1024]{0,1:T(8,128)S(1)} %get-tuple-element.27), channel_id=1, source_target_pairs={{3,0},{4,1},{5,2},{6,3},{7,4},{8,5},{9,6},{10,7},{11,8},{12,9},{13... | collective-permute-start | bytes 3145736 | tf_op jit(solution)/shard_map/ppermute | solution.py:50
  217.3 64.1 %collective-permute-start.12 = (f32[256,1024]{0,1:T(8,128)S(1)}, f32[256,1024]{0,1:T(8,128)S(1)}, u32[]{:S(2)}, u32[]{:S(2)}) collective-permute-start(f32[256,1024]{0,1:T(8,128)S(1)} %get-tuple-element.26), channel_id=1, source_target_pairs={{2,0},{3,1},{4,2},{5,3},{6,4},{7,5},{8,6},{9,7},{10,8},{11,9},{12,... | collective-permute-start | bytes 3145736 | tf_op jit(solution)/shard_map/ppermute | solution.py:50
  218.6 62.8 %collective-permute-start.11 = (f32[256,1024]{0,1:T(8,128)S(1)}, f32[256,1024]{0,1:T(8,128)S(1)}, u32[]{:S(2)}, u32[]{:S(2)}) collective-permute-start(f32[256,1024]{0,1:T(8,128)S(1)} %get-tuple-element.25), channel_id=1, source_target_pairs={{1,0},{2,1},{3,2},{4,3},{5,4},{6,5},{7,6},{8,7},{9,8},{10,9},{11,1... | collective-permute-start | bytes 3145736 | tf_op jit(solution)/shard_map/ppermute | solution.py:50
  282.1 0.8 copy-start.3
  306.9 2.6 copy-start.4
Sparse Core Ops, SparseCore 0:
  9.8 46.7 all-gather.1
  297.7 147.4 reduce-scatter.3
